TPU v7x, 32 devices: a whole 2x2x4 slice. The times are simulated.
32 devices in a mesh: gx: 8 (over z, x), gy: 4 (over y, core).
Axes of the slice: x: 2, y: 2, z: 4, core: 2. Of those that a mesh axis runs over, the one named last changes fastest.
Arguments:
- inputs: bfloat16 [3, 256, 8192], P(None, 'gy', 'gx'), may hold values from -600 to 600
- norm_gain: bfloat16 [8192], P('gx'), may hold values from 0.099609375 to 1.8984375
- query_weight: bfloat16 [8192, 8192], P('gx', 'gy'), may hold values from -0.0625 to 0.0625
- key_weight: bfloat16 [8192, 1024], P('gx', 'gy'), may hold values from -0.0625 to 0.0625
- value_weight: bfloat16 [8192, 1024], P('gx', 'gy'), may hold values from -0.0625 to 0.0625
- output_weight: bfloat16 [8192, 8192], P('gy', 'gx'), may hold values from -0.0625 to 0.0625
- query_down: bfloat16 [256, 8192, 64], P('gy', 'gx'), may hold values from -0.0625 to 0.0625
- query_up: bfloat16 [256, 64, 8192], P('gx', None, 'gy'), may hold values from -0.75 to 0.75
- output_down: bfloat16 [256, 8192, 64], P('gx', 'gy'), may hold values from -0.0625 to 0.0625
- output_up: bfloat16 [256, 64, 8192], P('gy', None, 'gx'), may hold values from -0.75 to 0.75
- block_adapter: int32 [2], replicated, may hold values from 0 to 255
- cache_lengths: int32 [256], P(('gx', 'gy')), may hold values from 1 to 256, as said below
- cache_keys: bfloat16 [256, 256, 1024], P(('gx', 'gy')), may hold values from -160 to 160
- cache_values: bfloat16 [256, 256, 1024], P(('gx', 'gy')), may hold values from -6 to 6
Outputs:
- block_output: bfloat16 [3, 256, 8192], P(None, 'gy', 'gx')
Inputs may be any that keep to these rules, and one draw needn't show every extreme that they name: `cache_lengths`: some request has exactly 256 cached positions.
All inputs are finite; a program needn't handle non-finite values.
Results may differ from a plain program's by a relative error of at most 0.012.
The roundings to bfloat16 on the way count: a program that leaves them out, or rounds other values in their place, can miss the bound.
Values may be sent and summed in bfloat16 or wider, within the bound.
No kernel may reach another device: no remote copies, remote signals or barrier semaphores. Data moves between devices by JAX's collectives and lax.ppermute only.
A program may use at most 192 MiB of HBM per device.

v0:
```python
import jax
import jax.numpy as jnp
from jax import lax
from jax.sharding import PartitionSpec as P

D = 8192
QUERY_HEADS = 64
KEY_VALUE_HEADS = 8
HEAD_FEATURES = 128
BLOCK = 128
STEPS = 3
EPS = 1e-05
THETA = 500000.0


def rotary_embedding(values_in, token_positions):
    half_size = values_in.shape[-1] // 2
    exponent = jnp.arange(half_size, dtype=jnp.float32) * 2.0 / values_in.shape[-1]
    frequency = THETA ** (-exponent)
    angles = token_positions.astype(jnp.float32)[:, None] * frequency[None, :]
    cosine = jnp.cos(angles)[:, None, :]
    sine_part = jnp.sin(angles)[:, None, :]
    lower = values_in[..., :half_size]
    upper = values_in[..., half_size:]
    return jnp.concatenate(
        [lower * cosine - upper * sine_part, upper * cosine + lower * sine_part], axis=-1
    )


def pick_adapters(table, adapter_ids, first_id):
    table_count = table.shape[0]
    wanted = first_id + jnp.arange(table_count, dtype=jnp.int32)
    onehot = (adapter_ids[:, None] == wanted[None, :]).astype(table.dtype)
    flat_table = table.reshape(table_count, -1)
    picked = jnp.dot(onehot, flat_table, preferred_element_type=jnp.float32).astype(table.dtype)
    return picked.reshape((adapter_ids.shape[0],) + table.shape[1:])


def attend(
    query_rows, previous_keys, previous_values, incoming_keys, incoming_values, lengths, step_index
):
    count_of_rows = query_rows.shape[0]
    context_window = previous_keys.shape[1]
    grouped_heads = query_rows.reshape(
        count_of_rows, KEY_VALUE_HEADS, QUERY_HEADS // KEY_VALUE_HEADS, HEAD_FEATURES
    )
    keys_previous = previous_keys.reshape(
        count_of_rows, context_window, KEY_VALUE_HEADS, HEAD_FEATURES
    )
    values_previous = previous_values.reshape(
        count_of_rows, context_window, KEY_VALUE_HEADS, HEAD_FEATURES
    )
    keys_incoming = incoming_keys.reshape(count_of_rows, -1, KEY_VALUE_HEADS, HEAD_FEATURES)
    values_incoming = incoming_values.reshape(count_of_rows, -1, KEY_VALUE_HEADS, HEAD_FEATURES)
    factor = HEAD_FEATURES ** (-0.5)
    score_old = (
        jnp.einsum(
            "rhgd,rchd->rhgc", grouped_heads, keys_previous, preferred_element_type=jnp.float32
        )
        * factor
    )
    score_new = (
        jnp.einsum(
            "rhgd,rshd->rhgs", grouped_heads, keys_incoming, preferred_element_type=jnp.float32
        )
        * factor
    )
    live_old = (jnp.arange(context_window, dtype=jnp.int32)[None, :] < lengths[:, None])[
        :, None, None, :
    ]
    live_new = (jnp.arange(keys_incoming.shape[1], dtype=jnp.int32) <= step_index)[
        None, None, None, :
    ]
    score_old = jnp.where(live_old, score_old, -1e30)
    score_new = jnp.where(live_new, score_new, -1e30)
    peak_score = jnp.maximum(jnp.max(score_old, axis=-1), jnp.max(score_new, axis=-1))
    weight_old = jnp.where(live_old, jnp.exp(score_old - peak_score[..., None]), 0.0)
    weight_new = jnp.where(live_new, jnp.exp(score_new - peak_score[..., None]), 0.0)
    weight_sum = jnp.sum(weight_old, axis=-1) + jnp.sum(weight_new, axis=-1)
    mixed_out = jnp.einsum(
        "rhgc,rchd->rhgd",
        weight_old.astype(jnp.bfloat16),
        values_previous,
        preferred_element_type=jnp.float32,
    )
    mixed_out = mixed_out + jnp.einsum(
        "rhgs,rshd->rhgd",
        weight_new.astype(jnp.bfloat16),
        values_incoming,
        preferred_element_type=jnp.float32,
    )
    return (mixed_out / weight_sum[..., None]).reshape(count_of_rows, -1).astype(jnp.bfloat16)


def normalize(rows_in, squares, norm_scale):
    factor_rows = lax.rsqrt(squares / D + EPS)
    return (rows_in.astype(jnp.float32) * factor_rows[:, None] * norm_scale[None, :]).astype(
        jnp.bfloat16
    )


def local(
    inputs,
    norm_gain,
    query_weight,
    key_weight,
    value_weight,
    output_weight,
    query_down,
    query_up,
    output_down,
    output_up,
    block_adapter,
    cache_lengths,
    cache_keys,
    cache_values,
):
    across_second = lax.axis_size("gy")
    index_first = lax.axis_index("gx")
    index_second = lax.axis_index("gy")
    request_count = inputs.shape[1] * across_second
    local_rows = cache_keys.shape[0]
    block_count = block_adapter.shape[0]
    norm_scale = norm_gain.astype(jnp.float32)
    query_first = pick_adapters(query_down, block_adapter, index_second * query_down.shape[0])
    query_second = pick_adapters(query_up, block_adapter, index_first * query_up.shape[0])
    output_first = pick_adapters(output_down, block_adapter, index_first * output_down.shape[0])
    output_second = pick_adapters(output_up, block_adapter, index_second * output_up.shape[0])
    incoming_keys = jnp.zeros((local_rows, STEPS, cache_keys.shape[2]), jnp.bfloat16)
    incoming_values = jnp.zeros((local_rows, STEPS, cache_values.shape[2]), jnp.bfloat16)
    results = []
    for step_index in range(STEPS):
        own_inputs = inputs[step_index]
        rows_all = lax.all_gather(own_inputs, "gy", axis=0, tiled=True)
        squares = lax.psum(jnp.sum(jnp.square(rows_all.astype(jnp.float32)), axis=1), "gx")
        normed = normalize(rows_all, squares, norm_scale)
        blocked = normed.reshape(block_count, BLOCK, -1)
        rank_part = jnp.einsum(
            "bnd,bdr->bnr", blocked, query_first, preferred_element_type=jnp.float32
        )
        rank_query = lax.psum(rank_part, ("gx", "gy")).astype(jnp.bfloat16)
        delta_query = jnp.einsum(
            "bnr,bre->bne", rank_query, query_second, preferred_element_type=jnp.float32
        ).reshape(request_count, -1)
        part_query = jnp.dot(normed, query_weight, preferred_element_type=jnp.float32) + delta_query
        part_key = jnp.dot(normed, key_weight, preferred_element_type=jnp.float32)
        part_value = jnp.dot(normed, value_weight, preferred_element_type=jnp.float32)
        summed = (
            lax.psum_scatter(part_query, "gx", scatter_dimension=0, tiled=True),
            lax.psum_scatter(part_key, "gx", scatter_dimension=0, tiled=True),
            lax.psum_scatter(part_value, "gx", scatter_dimension=0, tiled=True),
        )
        query_full, key_complete, value_full = (
            lax.all_to_all(
                summed[0].astype(jnp.bfloat16), "gy", split_axis=0, concat_axis=1, tiled=True
            ),
            lax.all_to_all(
                summed[1].astype(jnp.bfloat16), "gy", split_axis=0, concat_axis=1, tiled=True
            ),
            lax.all_to_all(
                summed[2].astype(jnp.bfloat16), "gy", split_axis=0, concat_axis=1, tiled=True
            ),
        )
        token_positions = cache_lengths + step_index
        query_rot = rotary_embedding(
            query_full.astype(jnp.float32).reshape(local_rows, QUERY_HEADS, HEAD_FEATURES),
            token_positions,
        ).astype(jnp.bfloat16)
        key_rotated = rotary_embedding(
            key_complete.astype(jnp.float32).reshape(local_rows, KEY_VALUE_HEADS, HEAD_FEATURES),
            token_positions,
        ).astype(jnp.bfloat16)
        incoming_keys = incoming_keys.at[:, step_index].set(key_rotated.reshape(local_rows, -1))
        incoming_values = incoming_values.at[:, step_index].set(value_full)
        mixed_local = attend(
            query_rot.reshape(local_rows, -1),
            cache_keys,
            cache_values,
            incoming_keys,
            incoming_values,
            cache_lengths,
            step_index,
        )
        head_group = lax.all_to_all(mixed_local, "gy", split_axis=1, concat_axis=0, tiled=True)
        mixed_all = lax.all_gather(head_group, "gx", axis=0, tiled=True)
        rank_part_out = jnp.einsum(
            "bnq,bqr->bnr",
            mixed_all.reshape(block_count, BLOCK, -1),
            output_first,
            preferred_element_type=jnp.float32,
        )
        rank_output = lax.psum(rank_part_out, ("gx", "gy")).astype(jnp.bfloat16)
        delta_output = jnp.einsum(
            "bnr,bre->bne", rank_output, output_second, preferred_element_type=jnp.float32
        ).reshape(request_count, -1)
        partial_out = (
            jnp.dot(mixed_all, output_weight, preferred_element_type=jnp.float32) + delta_output
        )
        results.append(
            lax.psum_scatter(partial_out, "gy", scatter_dimension=0, tiled=True).astype(
                jnp.bfloat16
            )
        )
    return jnp.stack(results)


def solution(mesh):
    in_specs = (
        P(None, "gy", "gx"),
        P("gx"),
        P("gx", "gy"),
        P("gx", "gy"),
        P("gx", "gy"),
        P("gy", "gx"),
        P("gy", "gx", None),
        P("gx", None, "gy"),
        P("gx", "gy", None),
        P("gy", None, "gx"),
        P(),
        P(("gx", "gy")),
        P(("gx", "gy"), None, None),
        P(("gx", "gy"), None, None),
    )
    out_specs = P(None, "gy", "gx")
    return jax.shard_map(local, mesh=mesh, in_specs=in_specs, out_specs=out_specs, check_vma=False)
```

profile of v0, /device:TPU:0, one launch (start us, length us, event | category | flops | bytes accessed | tf_op | source)
XLA Modules:
  0.0 941.0 jit_solution(17731421883246101163)
XLA Ops:
  7.7 8.6 all-gather.2
  16.3 7.3 all-gather
  23.8 7.3 all-gather.1
  32.3 21.7 %all-reduce.4 = (f32[256]{0:T(256)S(1)}, f32[256]{0:T(256)S(1)}, f32[256]{0:T(256)S(1)}) all-reduce(f32[256]{0:T(256)S(1)} %fusion.66, f32[256]{0:T(256)S(1)} %fusion.69, f32[256]{0:T(256)S(1)} %fusion.72), channel_id=1, replica_groups=mesh['gx'=8,'gy'=4] {'gx'}, use_global_device_ids=true, to_apply=%region_1.0 | all-reduce | flops 768 | bytes 6144 | tf_op jit(solution)/shard_map/psum | solution.py:135
  64.5 11.4 %copy.109 = bf16[4,8,64,2048]{3,1,2,0:T(8,128)(2,1)} copy(bf16[4,8,64,2048]{3,2,1,0:T(8,128)(2,1)} %bitcast.289) | data formatting | bytes 16777216
  75.9 15.6 %copy.74 = bf16[64,1024,64]{2,1,0:T(8,128)(2,1)} copy(bf16[64,1024,64]{1,2,0:T(8,128)(2,1)} %param.32) | data formatting | bytes 16777216 | tf_op args[6]
  91.5 16.5 %reshape.597 = bf16[64,65536]{1,0:T(8,128)(2,1)} reshape(bf16[64,1024,64]{2,1,0:T(8,128)(2,1)} %copy.74) | data formatting | bytes 16777216 | tf_op jit(solution)/shard_map/reshape | solution.py:34
  114.1 4.7 convolution_convert_fusion.1
  118.7 40.4 %all-reduce.7 = (bf16[2,128,64]{1,2,0:T(8,128)(2,1)S(1)}, bf16[2,128,64]{1,2,0:T(8,128)(2,1)S(1)}, bf16[2,128,64]{1,2,0:T(8,128)(2,1)S(1)}) all-reduce(f32[2,128,64]{1,2,0:T(8,128)S(1)} %fusion.191, f32[2,128,64]{1,2,0:T(8,128)S(1)} %fusion.183, f32[2,128,64]{1,2,0:T(8,128)S(1)} %fusion.187), channel_id=1, replica_groups=mesh['gx'=8,'gy'=4] {'gx','gy'}, use_global_device_ids=true, to_apply=%region_26.27 | all-reduce | flops 49152 | bytes 294912 | tf_op jit(solution)/shard_map/psum | solution.py:141
  159.7 4.8 convolution_add_fusion.1
  165.1 4.9 convolution_add_fusion
  170.5 4.8 convolution_add_fusion.2
  181.6 60.8 %reduce-scatter.17.cloned.1.call-done = f32[32,256]{1,0:T(8,128)} async-done(((f32[256,256]{1,0:T(8,128)}), f32[32,256]{1,0:T(8,128)}) %reduce-scatter.17.cloned.1.call-update) | async-done | bytes 32784 | tf_op jit(solution)/shard_map/reduce_scatter | solution.py:151
  243.9 62.1 %reduce-scatter.25.cloned.1.call-done = f32[32,256]{1,0:T(8,128)} async-done(((f32[256,256]{1,0:T(8,128)}), f32[32,256]{1,0:T(8,128)}) %reduce-scatter.25.cloned.1.call-update) | async-done | bytes 32784 | tf_op jit(solution)/shard_map/reduce_scatter | solution.py:151
  307.3 62.1 %reduce-scatter.31.cloned.1.call-done = f32[32,256]{1,0:T(8,128)} async-done(((f32[256,256]{1,0:T(8,128)}), f32[32,256]{1,0:T(8,128)}) %reduce-scatter.31.cloned.1.call-update) | async-done | bytes 32784 | tf_op jit(solution)/shard_map/reduce_scatter | solution.py:150
  370.8 62.2 %reduce-scatter.33.cloned.1.call-done = f32[32,256]{1,0:T(8,128)} async-done(((f32[256,256]{1,0:T(8,128)}), f32[32,256]{1,0:T(8,128)}) %reduce-scatter.33.cloned.1.call-update) | async-done | bytes 32784 | tf_op jit(solution)/shard_map/reduce_scatter | solution.py:151
  462.6 40.5 %reduce-scatter.21.cloned.1.call-done = f32[32,2048]{1,0:T(8,128)} async-done(((f32[256,2048]{1,0:T(8,128)}), f32[32,2048]{1,0:T(8,128)}) %reduce-scatter.21.cloned.1.call-update) | async-done | bytes 262160 | tf_op jit(solution)/shard_map/reduce_scatter | solution.py:149
  508.1 65.3 %reduce-scatter.29.cloned.1.call-done = f32[32,2048]{1,0:T(8,128)} async-done(((f32[256,2048]{1,0:T(8,128)}), f32[32,2048]{1,0:T(8,128)}) %reduce-scatter.29.cloned.1.call-update) | async-done | bytes 262160 | tf_op jit(solution)/shard_map/reduce_scatter | solution.py:149
  575.0 68.6 %reduce-scatter.13.cloned.1.call-done = f32[32,2048]{1,0:T(8,128)} async-done(((f32[256,2048]{1,0:T(8,128)}), f32[32,2048]{1,0:T(8,128)}) %reduce-scatter.13.cloned.1.call-update) | async-done | bytes 262160 | tf_op jit(solution)/shard_map/reduce_scatter | solution.py:149
  677.0 7.7 all_to_all.174
  688.0 7.7 all_to_all.175
  699.3 7.7 all_to_all.176
  707.1 12.0 %copy.113 = bf16[8,8,64,1024]{3,1,2,0:T(8,128)(2,1)} copy(bf16[8,8,64,1024]{3,2,1,0:T(8,128)(2,1)} %bitcast.290) | data formatting | bytes 16777216
  719.1 15.8 %copy.83 = bf16[32,2048,64]{2,1,0:T(8,128)(2,1)} copy(bf16[32,2048,64]{1,2,0:T(8,128)(2,1)} %param.34) | data formatting | bytes 16777216 | tf_op args[8]
  734.9 15.9 %reshape.608 = bf16[32,131072]{1,0:T(8,128)(2,1)} reshape(bf16[32,2048,64]{2,1,0:T(8,128)(2,1)} %copy.83) | data formatting | bytes 16777216 | tf_op jit(solution)/shard_map/reshape | solution.py:34
  756.2 4.7 convolution_convert_fusion.2
  765.9 39.2 %all-gather.7.cloned.1.call-done = bf16[256,2048]{1,0:T(8,128)(2,1)} async-done(((bf16[32,2048]{1,0:T(8,128)(2,1)}), bf16[256,2048]{1,0:T(8,128)(2,1)}) %all-gather.7.cloned.1.call-update) | async-done | bytes 1048592 | tf_op jit(solution)/shard_map/all_gather | solution.py:185
  806.9 41.8 %all-reduce.8 = (bf16[2,128,64]{1,2,0:T(8,128)(2,1)S(1)}, bf16[2,128,64]{1,2,0:T(8,128)(2,1)S(1)}, bf16[2,128,64]{1,2,0:T(8,128)(2,1)S(1)}) all-reduce(f32[2,128,64]{1,2,0:T(8,128)S(1)} %fusion.194, f32[2,128,64]{1,2,0:T(8,128)S(1)} %fusion.190, f32[2,128,64]{1,2,0:T(8,128)S(1)} %fusion.186), channel_id=1, replica_groups=mesh['gx'=8,'gy'=4] {'gx','gy'}, use_global_device_ids=true, to_apply=%region_34.35 | all-reduce | flops 49152 | bytes 294912 | tf_op jit(solution)/shard_map/psum | solution.py:192
  859.0 4.7 convolution_add_fusion.5
  863.8 13.7 %reduce-scatter.35.cloned.1.call-done = f32[64,1024]{1,0:T(8,128)} async-done(((f32[256,1024]{1,0:T(8,128)}), f32[64,1024]{1,0:T(8,128)}) %reduce-scatter.35.cloned.1.call-update) | async-done | bytes 262160 | tf_op jit(solution)/shard_map/reduce_scatter | solution.py:200
  878.4 26.5 %reduce-scatter.27.cloned.1.call-done = f32[64,1024]{1,0:T(8,128)} async-done(((f32[256,1024]{1,0:T(8,128)}), f32[64,1024]{1,0:T(8,128)}) %reduce-scatter.27.cloned.1.call-update) | async-done | bytes 262160 | tf_op jit(solution)/shard_map/reduce_scatter | solution.py:200
  905.9 26.4 %reduce-scatter.19.cloned.1.call-done = f32[64,1024]{1,0:T(8,128)} async-done(((f32[256,1024]{1,0:T(8,128)}), f32[64,1024]{1,0:T(8,128)}) %reduce-scatter.19.cloned.1.call-update) | async-done | bytes 262160 | tf_op jit(solution)/shard_map/reduce_scatter | solution.py:200
  (190 shorter events, 133.1 us)
Async XLA Ops:
  6.5 48.9 %copy-start = (bf16[1024,256]{1,0:T(8,128)(2,1)S(1)}, bf16[1024,256]{1,0:T(8,128)(2,1)}, u32[]{:S(2)}) copy-start(bf16[1024,256]{1,0:T(8,128)(2,1)} %param.29) | copy-start | bytes 1572868
  6.5 25.7 %copy-start.9 = (bf16[1024]{0:T(1024)(128)(2,1)S(1)}, bf16[1024]{0:T(1024)(128)(2,1)}, u32[]{:S(2)}) copy-start(bf16[1024]{0:T(1024)(128)(2,1)} %param.27) | copy-start | bytes 6148
  6.5 169.1 %reduce-scatter.15.cloned.1.call-start = ((), (), s32[]{:S(2)}) async-start(), calls=%async_computation.25 | async-start | bytes 294912 | tf_op jit(solution)/shard_map/reduce_scatter | solution.py:150
  55.4 7.5 copy-start.4
  56.5 123.8 %reduce-scatter.23.cloned.1.call-start = ((), (), s32[]{:S(2)}) async-start(), calls=%async_computation.30 | async-start | bytes 294912 | tf_op jit(solution)/shard_map/reduce_scatter | solution.py:150
  57.5 185.0 %reduce-scatter.17.cloned.1.call-start = ((), (), s32[]{:S(2)}) async-start(), calls=%async_computation.26 | async-start | bytes 294912 | tf_op jit(solution)/shard_map/reduce_scatter | solution.py:151
  59.7 246.3 %reduce-scatter.25.cloned.1.call-start = ((), (), s32[]{:S(2)}) async-start(), calls=%async_computation.31 | async-start | bytes 294912 | tf_op jit(solution)/shard_map/reduce_scatter | solution.py:151
  61.8 307.7 %reduce-scatter.31.cloned.1.call-start = ((), (), s32[]{:S(2)}) async-start(), calls=%async_computation.35 | async-start | bytes 294912 | tf_op jit(solution)/shard_map/reduce_scatter | solution.py:150
  62.9 370.1 %reduce-scatter.33.cloned.1.call-start = ((), (), s32[]{:S(2)}) async-start(), calls=%async_computation.36 | async-start | bytes 294912 | tf_op jit(solution)/shard_map/reduce_scatter | solution.py:151
  63.9 439.2 %reduce-scatter.21.cloned.1.call-start = ((), (), s32[]{:S(2)}) async-start(), calls=%async_computation.29 | async-start | bytes 2359296 | tf_op jit(solution)/shard_map/reduce_scatter | solution.py:149
  91.5 16.5 %copy-start.8 = (s32[2]{0:T(128)S(1)}, s32[2]{0:T(128)}, u32[]{:S(2)}) copy-start(s32[2]{0:T(128)} %param.36) | copy-start | bytes 28
  164.5 408.9 %reduce-scatter.29.cloned.1.call-start = ((), (), s32[]{:S(2)}) async-start(), calls=%async_computation.34 | async-start | bytes 2359296 | tf_op jit(solution)/shard_map/reduce_scatter | solution.py:149
  169.9 473.7 %reduce-scatter.13.cloned.1.call-start = ((), (), s32[]{:S(2)}) async-start(), calls=%async_computation.24 | async-start | bytes 2359296 | tf_op jit(solution)/shard_map/reduce_scatter | solution.py:149
  177.0 257.3 %all-to-all-start.1 = ((bf16[4,8,256]{2,1,0:T(8,128)(2,1)}), bf16[4,8,256]{2,1,0:T(8,128)(2,1)S(1)}, u32[]{:S(2)}, u32[]{:S(2)}) async-start(bf16[4,8,256]{2,1,0:T(8,128)(2,1)} %convert_bitcast_fusion.15), calls=%async_computation.3 | async-start | bytes 32768 | tf_op jit(solution)/shard_map/all_to_all | solution.py:157
  434.3 7.1 all-to-all-start.5
  441.4 7.1 all-to-all-start.9
  448.5 7.1 all-to-all-start.2
  455.6 7.1 all-to-all-start.6
  504.8 140.5 %all-to-all-start.4 = ((bf16[4,8,2048]{2,1,0:T(8,128)(2,1)}), bf16[4,8,2048]{2,1,0:T(8,128)(2,1)S(1)}, u32[]{:S(2)}, u32[]{:S(2)}) async-start(bf16[4,8,2048]{2,1,0:T(8,128)(2,1)} %convert_bitcast_fusion.6), calls=%async_computation.9 | async-start | bytes 262144 | tf_op jit(solution)/shard_map/all_to_all | solution.py:154
  645.3 7.9 all-to-all-start.8
  653.2 9.9 %all-to-all-start.10 = ((bf16[4,8,256]{2,1,0:T(8,128)(2,1)}), bf16[4,8,256]{2,1,0:T(8,128)(2,1)S(1)}, u32[]{:S(2)}, u32[]{:S(2)}) async-start(bf16[4,8,256]{2,1,0:T(8,128)(2,1)} %convert_bitcast_fusion.10), calls=%async_computation.21 | async-start | bytes 32768 | tf_op jit(solution)/shard_map/all_to_all | solution.py:160
  663.1 7.9 all-to-all-start
  666.4 94.4 %all-gather.11.cloned.1.call-start = ((), (), s32[]{:S(2)}) async-start(), calls=%async_computation.37 | async-start | bytes 1179648 | tf_op jit(solution)/shard_map/all_gather | solution.py:185
  684.7 79.5 %all-gather.9.cloned.1.call-start = ((), (), s32[]{:S(2)}) async-start(), calls=%async_computation.32 | async-start | bytes 1179648 | tf_op jit(solution)/shard_map/all_gather | solution.py:185
  695.7 109.4 %all-gather.7.cloned.1.call-start = ((), (), s32[]{:S(2)}) async-start(), calls=%async_computation.27 | async-start | bytes 1179648 | tf_op jit(solution)/shard_map/all_gather | solution.py:185
  707.0 170.4 %reduce-scatter.35.cloned.1.call-start = ((), (), s32[]{:S(2)}) async-start(), calls=%async_computation.38 | async-start | bytes 1310720 | tf_op jit(solution)/shard_map/reduce_scatter | solution.py:200
  760.9 88.2 %copy-start.5 = (bf16[256,2048]{1,0:T(8,128)(2,1)S(1)}, bf16[256,2048]{1,0:T(8,128)(2,1)}, u32[]{:S(2)}) copy-start(bf16[256,2048]{1,0:T(8,128)(2,1)} %all-gather.11.cloned.1.call-done) | copy-start | bytes 3145732
  849.0 4.9 copy-start.6
  853.6 51.4 %reduce-scatter.27.cloned.1.call-start = ((), (), s32[]{:S(2)}) async-start(), calls=%async_computation.33 | async-start | bytes 1310720 | tf_op jit(solution)/shard_map/reduce_scatter | solution.py:200
  854.0 5.0 copy-start.7
  858.6 73.7 %reduce-scatter.19.cloned.1.call-start = ((), (), s32[]{:S(2)}) async-start(), calls=%async_computation.28 | async-start | bytes 1310720 | tf_op jit(solution)/shard_map/reduce_scatter | solution.py:200
  859.0 75.0 %copy-start.1 = (bf16[1024,256]{1,0:T(8,128)(2,1)S(1)}, bf16[1024,256]{1,0:T(8,128)(2,1)}, u32[]{:S(2)}) copy-start(bf16[1024,256]{1,0:T(8,128)(2,1)} %param.29) | copy-start | bytes 1572868
  (4 other events, 14.7 us)
Sparse Core Ops, SparseCore 0:
  56.6 58.5 reduce-scatter.14
  118.5 60.3 reduce-scatter.22
  182.2 60.2 reduce-scatter.16
  245.7 60.2 reduce-scatter.24
  309.2 60.2 reduce-scatter.30
  372.6 60.2 reduce-scatter.32
  436.5 66.6 reduce-scatter.20
  506.7 66.6 reduce-scatter.28
  576.9 66.6 reduce-scatter.12
  684.8 38.2 all-gather.10
  725.3 38.8 all-gather.8
  766.2 38.8 all-gather.6
  853.7 23.7 reduce-scatter.34
  880.0 24.8 reduce-scatter.26
  907.3 24.9 reduce-scatter.18
where the time goes:
time: 947 us; the launch traced here: 941 us
  waiting for transfers between devices  552 us (58%)
  blocking collectives  150 us (16%)
  local copies, waits for them, and re-layouts  91.7 us (10%)
  matrix products  81.2 us (9%)
  starting transfers between devices  30.7 us (3%)
  other arithmetic  21.1 us (2%)
  between operations  14.5 us (2%)
    reduce_scatter x3, waiting for transfers between devices, local(): lax.psum_scatter(part_value, 'gx', scatter_dimension=0, tiled=True)  185 us
    reduce_scatter x3, waiting for transfers between devices, local(): lax.psum_scatter(part_query, 'gx', scatter_dimension=0, tiled=True)  174 us
    reduce_scatter x3, waiting for transfers between devices, local(): lax.psum_scatter(partial_out, 'gy', scatter_dimension=0, tiled=True)  66.6 us
    reduce_scatter x3, waiting for transfers between devices, local(): lax.psum_scatter(part_key, 'gx', scatter_dimension=0, tiled=True)  62.2 us
    unnamed x34, local copies, waits for them, and re-layouts  55.8 us
    psum x1, blocking collectives, local(): rank_output = lax.psum(rank_part_out, ('gx', 'gy')).astype(jnp.bfloat16)  41.8 us
    all_gather x3, waiting for transfers between devices, local(): mixed_all = lax.all_gather(head_group, 'gx', axis=0, tiled=True)  40.7 us
    psum x1, blocking collectives, local(): rank_query = lax.psum(rank_part, ('gx', 'gy')).astype(jnp.bfloat16)  40.4 us
  transfers between devices with their start and end apart: 24, of which 18 were waited for; matrix products, arithmetic and copies ran while one was open for 19% of the time, Pallas kernels for 0%

commit v1 on v0

--- a/solution.py
+++ b/solution.py
@@ -138,7 +138,7 @@
         rank_part = jnp.einsum(
             "bnd,bdr->bnr", blocked, query_first, preferred_element_type=jnp.float32
         )
-        rank_query = lax.psum(rank_part, ("gx", "gy")).astype(jnp.bfloat16)
+        rank_query = lax.psum(lax.psum(rank_part, "gy"), "gx").astype(jnp.bfloat16)
         delta_query = jnp.einsum(
             "bnr,bre->bne", rank_query, query_second, preferred_element_type=jnp.float32
         ).reshape(request_count, -1)

time: 947 us -> 1000 us (1.056)
  waiting for transfers between devices: 552 us -> 600 us
    reduce_scatter x3, waiting for transfers between devices: 62.2 us -> 99.8 us  [local(): lax.psum_scatter(part_key, 'gx', scatter_dimension=0, tiled=True)]
    unnamed x34 -> x36, local copies, waits for them, and re-layouts: 55.8 us -> 56.4 us
  transfers between devices with their start and end apart: 24 -> 25, of which waited for: 18 -> 20; matrix products, arithmetic and copies ran while one was open for 19% -> 14% of each run, Pallas kernels for 0% -> 0%
where the time goes in v1:
time: 1000 us; the launch traced here: 991 us
  waiting for transfers between devices  600 us (60%)
  blocking collectives  149 us (15%)
  local copies, waits for them, and re-layouts  92.4 us (9%)
  matrix products  81 us (8%)
  starting transfers between devices  30.7 us (3%)
  other arithmetic  21.2 us (2%)
  between operations  15.7 us (2%)
    reduce_scatter x3, waiting for transfers between devices, local(): lax.psum_scatter(part_value, 'gx', scatter_dimension=0, tiled=True)  188 us
    reduce_scatter x3, waiting for transfers between devices, local(): lax.psum_scatter(part_query, 'gx', scatter_dimension=0, tiled=True)  176 us
    reduce_scatter x3, waiting for transfers between devices, local(): lax.psum_scatter(part_key, 'gx', scatter_dimension=0, tiled=True)  99.8 us
    reduce_scatter x3, waiting for transfers between devices, local(): lax.psum_scatter(partial_out, 'gy', scatter_dimension=0, tiled=True)  66.8 us
    unnamed x36, local copies, waits for them, and re-layouts  56.4 us
    psum x1, blocking collectives, local(): rank_output = lax.psum(rank_part_out, ('gx', 'gy')).astype(jnp.bfloat16)  41.5 us
    all_gather x3, waiting for transfers between devices, local(): mixed_all = lax.all_gather(head_group, 'gx', axis=0, tiled=True)  41.3 us
    psum x1, blocking collectives, local(): rank_query = lax.psum(lax.psum(rank_part, 'gy'), 'gx').astype(jnp.bfloat16)  39.8 us
  transfers between devices with their start and end apart: 25, of which 20 were waited for; matrix products, arithmetic and copies ran while one was open for 14% of the time, Pallas kernels for 0%

profile of v1, /device:TPU:0, one launch (start us, length us, event | category | flops | bytes accessed | tf_op | source)
XLA Modules:
  0.0 990.7 jit_solution(10025358102399825124)
XLA Ops:
  8.5 8.6 all-gather.2
  17.2 7.3 all-gather
  25.4 7.3 all-gather.1
  33.9 21.7 %all-reduce.4 = (f32[256]{0:T(256)S(1)}, f32[256]{0:T(256)S(1)}, f32[256]{0:T(256)S(1)}) all-reduce(f32[256]{0:T(256)S(1)} %fusion.66, f32[256]{0:T(256)S(1)} %fusion.69, f32[256]{0:T(256)S(1)} %fusion.72), channel_id=1, replica_groups=mesh['gx'=8,'gy'=4] {'gx'}, use_global_device_ids=true, to_apply=%region_1.0 | all-reduce | flops 768 | bytes 6144 | tf_op jit(solution)/shard_map/psum | solution.py:135
  55.6 15.5 %copy.74 = bf16[64,1024,64]{2,1,0:T(8,128)(2,1)} copy(bf16[64,1024,64]{1,2,0:T(8,128)(2,1)} %param.32) | data formatting | bytes 16777216 | tf_op args[6]
  71.1 16.5 %reshape.597 = bf16[64,65536]{1,0:T(8,128)(2,1)} reshape(bf16[64,1024,64]{2,1,0:T(8,128)(2,1)} %copy.74) | data formatting | bytes 16777216 | tf_op jit(solution)/shard_map/reshape | solution.py:34
  104.3 11.4 %copy.109 = bf16[4,8,64,2048]{3,1,2,0:T(8,128)(2,1)} copy(bf16[4,8,64,2048]{3,2,1,0:T(8,128)(2,1)} %bitcast.289) | data formatting | bytes 16777216
  120.5 5.9 all-reduce.10.cloned.1.call-done
  126.3 39.8 %all-reduce.11 = (bf16[2,128,64]{1,2,0:T(8,128)(2,1)S(1)}, bf16[2,128,64]{1,2,0:T(8,128)(2,1)S(1)}, bf16[2,128,64]{1,2,0:T(8,128)(2,1)S(1)}) all-reduce(f32[2,128,64]{1,2,0:T(8,128)} %get-tuple-element.89, f32[2,128,64]{1,2,0:T(8,128)} %get-tuple-element.90, f32[2,128,64]{1,2,0:T(8,128)} %get-tuple-element.91), channel_id=1, replica_groups=mesh['gx'=8,'gy'=4] {'gx'}, use_global_device_ids=true, to_apply=%region_29.30 | all-reduce | flops 49152 | bytes 294912 | tf_op jit(solution)/shard_map/psum | solution.py:141
  166.7 4.8 convolution_add_fusion.1
  172.1 4.8 convolution_add_fusion
  177.6 4.8 convolution_add_fusion.2
  187.3 37.0 %reduce-scatter.23.cloned.1.call-done = f32[32,256]{1,0:T(8,128)} async-done(((f32[256,256]{1,0:T(8,128)}), f32[32,256]{1,0:T(8,128)}) %reduce-scatter.23.cloned.1.call-update) | async-done | bytes 32784 | tf_op jit(solution)/shard_map/reduce_scatter | solution.py:150
  225.6 62.6 %reduce-scatter.17.cloned.1.call-done = f32[32,256]{1,0:T(8,128)} async-done(((f32[256,256]{1,0:T(8,128)}), f32[32,256]{1,0:T(8,128)}) %reduce-scatter.17.cloned.1.call-update) | async-done | bytes 32784 | tf_op jit(solution)/shard_map/reduce_scatter | solution.py:151
  289.6 62.7 %reduce-scatter.25.cloned.1.call-done = f32[32,256]{1,0:T(8,128)} async-done(((f32[256,256]{1,0:T(8,128)}), f32[32,256]{1,0:T(8,128)}) %reduce-scatter.25.cloned.1.call-update) | async-done | bytes 32784 | tf_op jit(solution)/shard_map/reduce_scatter | solution.py:151
  353.7 62.8 %reduce-scatter.31.cloned.1.call-done = f32[32,256]{1,0:T(8,128)} async-done(((f32[256,256]{1,0:T(8,128)}), f32[32,256]{1,0:T(8,128)}) %reduce-scatter.31.cloned.1.call-update) | async-done | bytes 32784 | tf_op jit(solution)/shard_map/reduce_scatter | solution.py:150
  417.8 62.8 %reduce-scatter.33.cloned.1.call-done = f32[32,256]{1,0:T(8,128)} async-done(((f32[256,256]{1,0:T(8,128)}), f32[32,256]{1,0:T(8,128)}) %reduce-scatter.33.cloned.1.call-update) | async-done | bytes 32784 | tf_op jit(solution)/shard_map/reduce_scatter | solution.py:151
  510.4 40.9 %reduce-scatter.21.cloned.1.call-done = f32[32,2048]{1,0:T(8,128)} async-done(((f32[256,2048]{1,0:T(8,128)}), f32[32,2048]{1,0:T(8,128)}) %reduce-scatter.21.cloned.1.call-update) | async-done | bytes 262160 | tf_op jit(solution)/shard_map/reduce_scatter | solution.py:149
  556.3 65.7 %reduce-scatter.29.cloned.1.call-done = f32[32,2048]{1,0:T(8,128)} async-done(((f32[256,2048]{1,0:T(8,128)}), f32[32,2048]{1,0:T(8,128)}) %reduce-scatter.29.cloned.1.call-update) | async-done | bytes 262160 | tf_op jit(solution)/shard_map/reduce_scatter | solution.py:149
  623.7 68.9 %reduce-scatter.13.cloned.1.call-done = f32[32,2048]{1,0:T(8,128)} async-done(((f32[256,2048]{1,0:T(8,128)}), f32[32,2048]{1,0:T(8,128)}) %reduce-scatter.13.cloned.1.call-update) | async-done | bytes 262160 | tf_op jit(solution)/shard_map/reduce_scatter | solution.py:149
  725.9 7.7 all_to_all.174
  736.9 7.7 all_to_all.175
  748.2 7.7 all_to_all.176
  755.9 11.9 %copy.113 = bf16[8,8,64,1024]{3,1,2,0:T(8,128)(2,1)} copy(bf16[8,8,64,1024]{3,2,1,0:T(8,128)(2,1)} %bitcast.290) | data formatting | bytes 16777216
  767.9 15.8 %copy.83 = bf16[32,2048,64]{2,1,0:T(8,128)(2,1)} copy(bf16[32,2048,64]{1,2,0:T(8,128)(2,1)} %param.34) | data formatting | bytes 16777216 | tf_op args[8]
  783.6 15.9 %reshape.608 = bf16[32,131072]{1,0:T(8,128)(2,1)} reshape(bf16[32,2048,64]{2,1,0:T(8,128)(2,1)} %copy.83) | data formatting | bytes 16777216 | tf_op jit(solution)/shard_map/reshape | solution.py:34
  814.9 39.6 %all-gather.7.cloned.1.call-done = bf16[256,2048]{1,0:T(8,128)(2,1)} async-done(((bf16[32,2048]{1,0:T(8,128)(2,1)}), bf16[256,2048]{1,0:T(8,128)(2,1)}) %all-gather.7.cloned.1.call-update) | async-done | bytes 1048592 | tf_op jit(solution)/shard_map/all_gather | solution.py:185
  856.2 41.5 %all-reduce.12 = (bf16[2,128,64]{1,2,0:T(8,128)(2,1)S(1)}, bf16[2,128,64]{1,2,0:T(8,128)(2,1)S(1)}, bf16[2,128,64]{1,2,0:T(8,128)(2,1)S(1)}) all-reduce(f32[2,128,64]{1,2,0:T(8,128)S(1)} %fusion.194, f32[2,128,64]{1,2,0:T(8,128)S(1)} %fusion.190, f32[2,128,64]{1,2,0:T(8,128)S(1)} %fusion.186), channel_id=1, replica_groups=mesh['gx'=8,'gy'=4] {'gx','gy'}, use_global_device_ids=true, to_apply=%region_37.38 | all-reduce | flops 49152 | bytes 294912 | tf_op jit(solution)/shard_map/psum | solution.py:192
  908.1 4.7 convolution_add_fusion.5
  912.8 13.8 %reduce-scatter.35.cloned.1.call-done = f32[64,1024]{1,0:T(8,128)} async-done(((f32[256,1024]{1,0:T(8,128)}), f32[64,1024]{1,0:T(8,128)}) %reduce-scatter.35.cloned.1.call-update) | async-done | bytes 262160 | tf_op jit(solution)/shard_map/reduce_scatter | solution.py:200
  927.6 26.5 %reduce-scatter.27.cloned.1.call-done = f32[64,1024]{1,0:T(8,128)} async-done(((f32[256,1024]{1,0:T(8,128)}), f32[64,1024]{1,0:T(8,128)}) %reduce-scatter.27.cloned.1.call-update) | async-done | bytes 262160 | tf_op jit(solution)/shard_map/reduce_scatter | solution.py:200
  955.0 26.5 %reduce-scatter.19.cloned.1.call-done = f32[64,1024]{1,0:T(8,128)} async-done(((f32[256,1024]{1,0:T(8,128)}), f32[64,1024]{1,0:T(8,128)}) %reduce-scatter.19.cloned.1.call-update) | async-done | bytes 262160 | tf_op jit(solution)/shard_map/reduce_scatter | solution.py:200
  (195 shorter events, 143.7 us)
Async XLA Ops:
  7.4 89.9 %copy-start = (bf16[1024,256]{1,0:T(8,128)(2,1)S(1)}, bf16[1024,256]{1,0:T(8,128)(2,1)}, u32[]{:S(2)}) copy-start(bf16[1024,256]{1,0:T(8,128)(2,1)} %param.29) | copy-start | bytes 1572868
  7.4 26.6 %copy-start.10 = (bf16[1024]{0:T(1024)(128)(2,1)S(1)}, bf16[1024]{0:T(1024)(128)(2,1)}, u32[]{:S(2)}) copy-start(bf16[1024]{0:T(1024)(128)(2,1)} %param.27) | copy-start | bytes 6148
  7.4 119.0 %all-reduce.10.cloned.1.call-start = ((), (), s32[]{:S(2)}) async-start(), calls=%async_computation.39 | async-start | bytes 393216 | tf_op jit(solution)/shard_map/psum | solution.py:141
  71.1 16.6 %copy-start.9 = (s32[2]{0:T(128)S(1)}, s32[2]{0:T(128)}, u32[]{:S(2)}) copy-start(s32[2]{0:T(128)} %param.36) | copy-start | bytes 28
  94.3 5.1 copy-start.5
  97.2 85.4 %reduce-scatter.15.cloned.1.call-start = ((), (), s32[]{:S(2)}) async-start(), calls=%async_computation.25 | async-start | bytes 294912 | tf_op jit(solution)/shard_map/reduce_scatter | solution.py:150
  98.3 125.9 %reduce-scatter.23.cloned.1.call-start = ((), (), s32[]{:S(2)}) async-start(), calls=%async_computation.30 | async-start | bytes 294912 | tf_op jit(solution)/shard_map/reduce_scatter | solution.py:150
  99.4 188.9 %reduce-scatter.17.cloned.1.call-start = ((), (), s32[]{:S(2)}) async-start(), calls=%async_computation.26 | async-start | bytes 294912 | tf_op jit(solution)/shard_map/reduce_scatter | solution.py:151
  100.5 251.9 %reduce-scatter.25.cloned.1.call-start = ((), (), s32[]{:S(2)}) async-start(), calls=%async_computation.31 | async-start | bytes 294912 | tf_op jit(solution)/shard_map/reduce_scatter | solution.py:151
  101.6 314.9 %reduce-scatter.31.cloned.1.call-start = ((), (), s32[]{:S(2)}) async-start(), calls=%async_computation.35 | async-start | bytes 294912 | tf_op jit(solution)/shard_map/reduce_scatter | solution.py:150
  102.7 377.9 %reduce-scatter.33.cloned.1.call-start = ((), (), s32[]{:S(2)}) async-start(), calls=%async_computation.36 | async-start | bytes 294912 | tf_op jit(solution)/shard_map/reduce_scatter | solution.py:151
  103.8 447.6 %reduce-scatter.21.cloned.1.call-start = ((), (), s32[]{:S(2)}) async-start(), calls=%async_computation.29 | async-start | bytes 2359296 | tf_op jit(solution)/shard_map/reduce_scatter | solution.py:149
  171.5 450.5 %reduce-scatter.29.cloned.1.call-start = ((), (), s32[]{:S(2)}) async-start(), calls=%async_computation.34 | async-start | bytes 2359296 | tf_op jit(solution)/shard_map/reduce_scatter | solution.py:149
  176.9 515.6 %reduce-scatter.13.cloned.1.call-start = ((), (), s32[]{:S(2)}) async-start(), calls=%async_computation.24 | async-start | bytes 2359296 | tf_op jit(solution)/shard_map/reduce_scatter | solution.py:149
  184.0 298.0 %all-to-all-start.1 = ((bf16[4,8,256]{2,1,0:T(8,128)(2,1)}), bf16[4,8,256]{2,1,0:T(8,128)(2,1)S(1)}, u32[]{:S(2)}, u32[]{:S(2)}) async-start(bf16[4,8,256]{2,1,0:T(8,128)(2,1)} %convert_bitcast_fusion.15), calls=%async_computation.3 | async-start | bytes 32768 | tf_op jit(solution)/shard_map/all_to_all | solution.py:157
  482.0 7.1 all-to-all-start.5
  489.0 7.1 all-to-all-start.9
  496.1 7.3 all-to-all-start.2
  503.4 7.1 all-to-all-start.6
  553.0 141.1 %all-to-all-start.4 = ((bf16[4,8,2048]{2,1,0:T(8,128)(2,1)}), bf16[4,8,2048]{2,1,0:T(8,128)(2,1)S(1)}, u32[]{:S(2)}, u32[]{:S(2)}) async-start(bf16[4,8,2048]{2,1,0:T(8,128)(2,1)} %convert_bitcast_fusion.6), calls=%async_computation.9 | async-start | bytes 262144 | tf_op jit(solution)/shard_map/all_to_all | solution.py:154
  694.1 7.9 all-to-all-start.8
  702.1 9.9 all-to-all-start.10
  711.9 7.9 all-to-all-start
  715.3 94.3 %all-gather.11.cloned.1.call-start = ((), (), s32[]{:S(2)}) async-start(), calls=%async_computation.37 | async-start | bytes 1179648 | tf_op jit(solution)/shard_map/all_gather | solution.py:185
  733.6 79.6 %all-gather.9.cloned.1.call-start = ((), (), s32[]{:S(2)}) async-start(), calls=%async_computation.32 | async-start | bytes 1179648 | tf_op jit(solution)/shard_map/all_gather | solution.py:185
  744.5 109.9 %all-gather.7.cloned.1.call-start = ((), (), s32[]{:S(2)}) async-start(), calls=%async_computation.27 | async-start | bytes 1179648 | tf_op jit(solution)/shard_map/all_gather | solution.py:185
  755.9 170.7 %reduce-scatter.35.cloned.1.call-start = ((), (), s32[]{:S(2)}) async-start(), calls=%async_computation.38 | async-start | bytes 1310720 | tf_op jit(solution)/shard_map/reduce_scatter | solution.py:200
  809.6 88.5 %copy-start.6 = (bf16[256,2048]{1,0:T(8,128)(2,1)S(1)}, bf16[256,2048]{1,0:T(8,128)(2,1)}, u32[]{:S(2)}) copy-start(bf16[256,2048]{1,0:T(8,128)(2,1)} %all-gather.11.cloned.1.call-done) | copy-start | bytes 3145732
  902.7 51.4 %reduce-scatter.27.cloned.1.call-start = ((), (), s32[]{:S(2)}) async-start(), calls=%async_computation.33 | async-start | bytes 1310720 | tf_op jit(solution)/shard_map/reduce_scatter | solution.py:200
  903.1 5.0 copy-start.8
  907.7 73.9 %reduce-scatter.19.cloned.1.call-start = ((), (), s32[]{:S(2)}) async-start(), calls=%async_computation.28 | async-start | bytes 1310720 | tf_op jit(solution)/shard_map/reduce_scatter | solution.py:200
  908.1 75.3 %copy-start.1 = (bf16[1024,256]{1,0:T(8,128)(2,1)S(1)}, bf16[1024,256]{1,0:T(8,128)(2,1)}, u32[]{:S(2)}) copy-start(bf16[1024,256]{1,0:T(8,128)(2,1)} %param.29) | copy-start | bytes 1572868
  (6 other events, 20.6 us)
Sparse Core Ops, SparseCore 0:
  97.3 28.9 all-reduce.9
  902.8 23.7 reduce-scatter.34
  929.1 24.9 reduce-scatter.26
  956.6 24.8 reduce-scatter.18
Sparse Core Ops, SparseCore 1:
  101.4 58.7 reduce-scatter.14
  163.7 60.5 reduce-scatter.22
  227.8 60.4 reduce-scatter.16
  292.0 60.3 reduce-scatter.24
  356.1 60.4 reduce-scatter.30
  420.2 60.4 reduce-scatter.32
  484.4 66.9 reduce-scatter.20
  555.2 66.8 reduce-scatter.28
  625.8 66.6 reduce-scatter.12
  733.7 38.3 all-gather.10
  774.2 38.9 all-gather.8
  815.5 38.9 all-gather.6
